TPU v7x, 32 devices: a whole 2x2x4 slice. The times are simulated.
32 devices in a mesh: grp: 2 (over y), cell: 8 (over z, x), gene: 2 (over core).
Axes of the slice: x: 2, y: 2, z: 4, core: 2. Of those that a mesh axis runs over, the one named last changes fastest.
Arguments:
- expression: bfloat16 [2048, 16384], P(('grp', 'cell'), 'gene'), parts along dimension 0, may hold values from -6 to 6
- design: bfloat16 [2048, 128], P(('grp', 'cell')), parts along dimension 0, may hold values from -24 to 24
- quantile_level: float32 [16384], P('gene'), may hold values from 0.1 to 0.9
Outputs:
- quantile_slack: bfloat16 [2048, 16384], P(('grp', 'cell'), 'gene'), parts along dimension 0
- low_rank_coef: float32 [32768, 128], P(('grp', 'gene', 'cell')), parts along dimension 0
There are 2 independent parts, one for each index of `grp`. A program takes and returns all parts, laid end to end along the dimension named above; an argument that names none is the same for every part. Nothing has to cross between parts.
All inputs are finite; a program needn't handle non-finite values.
Results may differ from a plain program's by a relative error of at most 0.0025.
The roundings to bfloat16 on the way count: a program that leaves them out, or rounds other values in their place, can miss the bound.
Values may be sent and summed in bfloat16 or wider, within the bound.
No kernel may reach another device: no remote copies, remote signals or barrier semaphores. Data moves between devices by JAX's collectives and lax.ppermute only.
A program may use at most 64 MiB of HBM per device.

v0:
```python
import math
import jax
import jax.numpy as jnp
from jax import lax
from jax.sharding import PartitionSpec as P

NS_STEPS = 8
shrink_rate = 0.25


def matmul(left, right):
    return jnp.dot(left, right, precision=lax.Precision.HIGHEST)


def invert(matrix):
    identity = jnp.eye(matrix.shape[0], dtype=jnp.float32)
    factor = jnp.linalg.cholesky(matrix)
    lower_inv = lax.linalg.triangular_solve(factor, identity, left_side=True, lower=True)
    return matmul(lower_inv.T, lower_inv)


def newton(moment):
    identity = jnp.eye(moment.shape[0], dtype=jnp.float32)
    current = moment / jnp.trace(moment)
    root_inv = identity
    for sweep in range(NS_STEPS):
        middle = 1.5 * identity - 0.5 * matmul(root_inv, current)
        current = matmul(current, middle)
        root_inv = matmul(middle, root_inv)
    return root_inv


def per_device(expression, design, quantile_level):
    width = design.shape[1]
    identity = jnp.eye(width, dtype=jnp.float32)
    local_gram = lax.dot_general(
        design, design, (((0,), (0,)), ((), ())), preferred_element_type=jnp.float32
    )
    crossed = lax.psum_scatter(
        lax.dot_general(
            expression, design, (((0,), (0,)), ((), ())), preferred_element_type=jnp.float32
        ),
        "cell",
        scatter_dimension=0,
        tiled=True,
    )
    gram_total = lax.psum(local_gram, "cell")
    inverse = invert(gram_total + identity)
    coef = matmul(crossed, inverse)
    local_moment = lax.dot_general(
        coef, coef, (((0,), (0,)), ((), ())), precision=lax.Precision.HIGHEST
    )
    moment = lax.psum(local_moment, ("cell", "gene"))
    root_inv = newton(moment)
    low_rank_coef = coef - shrink_rate / math.sqrt(width) * matmul(coef, root_inv)
    coef_low = coef.astype(jnp.bfloat16)
    fitted = lax.dot_general(
        design,
        lax.all_gather(coef_low, "cell", axis=0, tiled=True),
        (((1,), (1,)), ((), ())),
        preferred_element_type=jnp.float32,
    )
    slack = expression.astype(jnp.float32) - fitted
    level = quantile_level[None, :]
    quantile_slack = (slack - jnp.clip(slack, level - 1.0, level)).astype(jnp.bfloat16)
    return (quantile_slack, low_rank_coef)


def solution(mesh):
    placed = (P(("grp", "cell"), "gene"), P(("grp", "cell"), None), P("gene"))
    return jax.shard_map(
        per_device,
        mesh=mesh,
        in_specs=placed,
        out_specs=(P(("grp", "cell"), "gene"), P(("grp", "gene", "cell"), None)),
        check_vma=False,
    )
```

profile of v0, /device:TPU:0, one launch (start us, length us, event | category | flops | bytes accessed | tf_op | source)
XLA Modules:
  0.0 335.5 jit_solution(2231902465308282045)
XLA Ops:
  7.2 0.7 copy-done
  7.9 0.8 fusion.18
  8.8 4.3 %fusion.17 = f32[8192,128]{1,0:T(8,128)} fusion(bf16[128,8192]{1,0:T(8,128)(2,1)} %param.3, bf16[128,128]{1,0:T(8,128)(2,1)S(1)} %copy-done), kind=kOutput, calls=%fused_computation.38 | convolution fusion | flops 268435456 | bytes 6324224 | tf_op jit(solution)/shard_map/dot_general | solution.py:40
  13.4 70.6 %all-reduce.3.cloned.1.call-done = f32[128,128]{0,1:T(8,128)} async-done(((f32[128,128]{0,1:T(8,128)}), f32[128,128]{0,1:T(8,128)}) %all-reduce.3.cloned.1.call-update) | async-done | bytes 65552 | tf_op jit(solution)/shard_map/psum | solution.py:47
  84.0 0.8 convert_add_fusion
  84.9 11.7 %cholesky.29 = f32[128,128]{1,0:T(8,128)S(1)} custom-call(f32[128,128]{1,0:T(8,128)S(1)} %fusion.13), custom_call_target="Cholesky" | custom-call | tf_op jit(solution)/shard_map/jit(cholesky)/cholesky | solution.py:17
  96.7 0.6 compare_reduce_fusion
  97.3 0.7 fusion.10
  98.0 9.8 %custom-call.6 = f32[1,128,128]{1,2,0:T(8,128)S(1)} custom-call(f32[1,128,128]{2,1,0:T(8,128)S(1)} %fusion.10), custom_call_target="InvertDiagBlocksLowerTriangular" | custom-call | tf_op jit(solution)/shard_map/triangular_solve | solution.py:18
  107.8 0.2 fusion.11
  108.0 0.3 fusion.19
  108.3 67.6 %reduce-scatter.2.cloned.1.call-done = f32[1024,128]{1,0:T(8,128)} async-done(((f32[8192,128]{1,0:T(8,128)}), f32[1024,128]{1,0:T(8,128)}) %reduce-scatter.2.cloned.1.call-update) | async-done | bytes 524304 | tf_op jit(solution)/shard_map/reduce_scatter | solution.py:39
  176.0 2.3 fusion.16
  178.3 1.6 fusion.20
  180.0 0.2 all-gather.2.cloned.1.call-start
  180.2 2.4 copy.5
  182.7 83.3 %all-reduce.5.cloned.1.call-done = f32[128,128]{1,0:T(8,128)} async-done(((f32[128,128]{1,0:T(8,128)}), f32[128,128]{1,0:T(8,128)}) %all-reduce.5.cloned.1.call-update) | async-done | bytes 65552 | tf_op jit(solution)/shard_map/psum | solution.py:53
  266.0 1.5 select_reduce_fusion
  267.5 1.7 fusion.9
  269.3 1.7 fusion.15
  271.0 0.2 fusion.8
  271.2 0.2 fusion.21
  271.7 0.2 fusion.7
  271.9 0.2 fusion.23
  272.7 0.2 fusion.26
  273.2 0.2 fusion.27
  273.4 0.2 fusion.28
  274.0 0.2 fusion.30
  275.3 1.4 fusion.1
  276.6 42.0 %all-gather.2.cloned.1.call-done = bf16[8192,128]{1,0:T(8,128)(2,1)} async-done(((bf16[1024,128]{1,0:T(8,128)(2,1)}), bf16[8192,128]{1,0:T(8,128)(2,1)}) %all-gather.2.cloned.1.call-update) | async-done | bytes 2097168 | tf_op jit(solution)/shard_map/all_gather | solution.py:59
  318.7 6.2 %subtract_convert_fusion = bf16[128,8192]{0,1:T(8,128)(2,1)} fusion(bf16[8192,128]{1,0:T(8,128)(2,1)} %all-gather.2.cloned.1.call-done, bf16[128,128]{1,0:T(8,128)(2,1)S(1)} %copy-done, bf16[128,8192]{0,1:T(8,128)(2,1)S(1)} %copy-done.2, f32[8192]{0:T(1024)S(1)} %broadcast_add_fusion, f32[8192]{0:T(1024)S(1)} %copy-done.3), kind=kOutput, calls=%fused_computation.2 | convolution fusion | flops 274726912 | bytes 6389760 | tf_op jit(solution)/shard_map/dot_general | solution.py:57
  324.9 4.1 %copy.9 = bf16[128,8192]{1,0:T(8,128)(2,1)} copy(bf16[128,8192]{0,1:T(8,128)(2,1)} %subtract_convert_fusion) | data formatting | bytes 4194304
  (33 shorter events, 3.1 us)
Async XLA Ops:
  7.2 0.8 copy-start
  7.2 76.8 %all-reduce.3.cloned.1.call-start = ((), (), s32[]{:S(2)}) async-start(), calls=%async_computation.2 | async-start | bytes 131072 | tf_op jit(solution)/shard_map/psum | solution.py:47
  8.8 167.2 %reduce-scatter.2.cloned.1.call-start = ((), (), s32[]{:S(2)}) async-start(), calls=%async_computation.1 | async-start | bytes 4718592 | tf_op jit(solution)/shard_map/reduce_scatter | solution.py:39
  13.1 167.0 %copy-start.3 = (f32[8192]{0:T(1024)S(1)}, f32[8192]{0:T(1024)}, u32[]{:S(2)}) copy-start(f32[8192]{0:T(1024)} %param.5) | copy-start | bytes 98308
  13.2 167.1 %copy-start.1 = (bf16[128,8192]{1,0:T(8,128)(2,1)S(1)}, bf16[128,8192]{1,0:T(8,128)(2,1)}, u32[]{:S(2)}) copy-start(bf16[128,8192]{1,0:T(8,128)(2,1)} %param.3) | copy-start | bytes 6291460
  13.2 252.8 %all-reduce.5.cloned.1.call-start = ((), (), s32[]{:S(2)}) async-start(), calls=%async_computation.4 | async-start | bytes 131072 | tf_op jit(solution)/shard_map/psum | solution.py:53
  180.0 138.7 %all-gather.2.cloned.1.call-start = ((), (), s32[]{:S(2)}) async-start(), calls=%async_computation.3 | async-start | bytes 2359296 | tf_op jit(solution)/shard_map/all_gather | solution.py:59
  271.9 46.8 %copy-start.2 = (bf16[128,8192]{0,1:T(8,128)(2,1)S(1)}, bf16[128,8192]{0,1:T(8,128)(2,1)}, u32[]{:S(2)}) copy-start(bf16[128,8192]{0,1:T(8,128)(2,1)} %copy.5) | copy-start | bytes 6291460
Sparse Core Ops, SparseCore 0:
  12.0 71.9 all-reduce.2
  87.6 88.3 reduce-scatter.1
  180.1 85.8 all-reduce.4
  268.0 50.6 all-gather.1
where the time goes:
time: 336 us; the launch traced here: 335 us
  waiting for transfers between devices  264 us (79%)
  other arithmetic  25.2 us (8%)
  matrix products  24.8 us (7%)
  between operations  14 us (4%)
  local copies, waits for them, and re-layouts  7.44 us (2%)
    psum x1, waiting for transfers between devices, per_device(): moment = lax.psum(local_moment, ('cell', 'gene'))  83.3 us
    psum x1, waiting for transfers between devices, per_device(): gram_total = lax.psum(local_gram, 'cell')  70.6 us
    reduce_scatter x1, waiting for transfers between devices, per_device(): lax.psum_scatter(lax.dot_general(expression, design, (((0,), (0,)), ((),...  67.6 us
    all_gather x1, waiting for transfers between devices, per_device(): lax.all_gather(coef_low, 'cell', axis=0, tiled=True)  42 us
    another operation x4, other arithmetic, invert(): factor = jnp.linalg.cholesky(matrix)  12.4 us
    dot_general x26, matrix products, matmul(): return jnp.dot(left, right, precision=lax.Precision.HIGHEST)  11.6 us
    another operation x2, other arithmetic, invert(): lax.linalg.triangular_solve(factor, identity, left_side=True, lower=True)  10.5 us
    unnamed x10, local copies, waits for them, and re-layouts  7.23 us
  transfers between devices with their start and end apart: 4, of which 4 were waited for; matrix products, arithmetic and copies ran while one was open for 12% of the time, Pallas kernels for 0%

commit v1 on v0

--- a/solution.py
+++ b/solution.py
@@ -54,9 +54,24 @@
     root_inv = newton(moment)
     low_rank_coef = coef - shrink_rate / math.sqrt(width) * matmul(coef, root_inv)
     coef_low = coef.astype(jnp.bfloat16)
+
+    def lay_the_joints(raw, axis_no):
+        named_axis = "cell"
+        o_now = jax.lax.axis_size(named_axis)
+        clean, p_next, x_next = (o_now, jax.lax.axis_index(named_axis), raw.shape[axis_no])
+        all_values, reached = (raw, 1)
+        while reached < clean:
+            samples = []
+            for q in [*range(clean)]:
+                samples.append((q, (q - reached) % clean))
+            far_arr = jax.lax.ppermute(all_values, axis_name=named_axis, perm=samples)
+            all_values = jnp.concatenate([all_values, far_arr], axis=axis_no)
+            reached = 2 * reached
+        return jnp.roll(all_values, p_next * x_next, axis=axis_no)
+
     fitted = lax.dot_general(
         design,
-        lax.all_gather(coef_low, "cell", axis=0, tiled=True),
+        lay_the_joints(coef_low, 0),
         (((1,), (1,)), ((), ())),
         preferred_element_type=jnp.float32,
     )

time: 336 us -> 350 us (1.042)
  starting transfers between devices: 0.34 us -> 10.7 us
  waiting for transfers between devices: 264 us -> 269 us
    ppermute x0 -> x3, waiting for transfers between devices: none -> 49.6 us  [lay_the_joints(): far_arr = jax.lax.ppermute(all_values, axis_name=named_axis, perm=samples)]
    all_gather x1 -> x0, waiting for transfers between devices: 42 us -> none  [per_device(): lax.all_gather(coef_low, 'cell', axis=0, tiled=True)]
    ppermute x0 -> x3, starting transfers between devices: none -> 10.6 us  [lay_the_joints(): far_arr = jax.lax.ppermute(all_values, axis_name=named_axis, perm=samples)]
    unnamed x10 -> x18, local copies, waits for them, and re-layouts: 7.23 us -> 6.44 us
  transfers between devices with their start and end apart: 4 -> 6, of which waited for: 4 -> 5; matrix products, arithmetic and copies ran while one was open for 12% -> 12% of each run, Pallas kernels for 0% -> 0%
where the time goes in v1:
time: 350 us
  waiting for transfers between devices  269 us (77%)
  other arithmetic  25.3 us (7%)
  matrix products  23.9 us (7%)
  between operations  14.1 us (4%)
  starting transfers between devices  10.7 us (3%)
  local copies, waits for them, and re-layouts  6.78 us (2%)
    psum x1, waiting for transfers between devices, per_device(): moment = lax.psum(local_moment, ('cell', 'gene'))  81.3 us
    psum x1, waiting for transfers between devices, per_device(): gram_total = lax.psum(local_gram, 'cell')  70.6 us
    reduce_scatter x1, waiting for transfers between devices, per_device(): lax.psum_scatter(lax.dot_general(expression, design, (((0,), (0,)), ((),...  67.6 us
    ppermute x3, waiting for transfers between devices, lay_the_joints(): far_arr = jax.lax.ppermute(all_values, axis_name=named_axis, perm=samples)  49.6 us
    another operation x4, other arithmetic, invert(): factor = jnp.linalg.cholesky(matrix)  12.4 us
    dot_general x26, matrix products, matmul(): return jnp.dot(left, right, precision=lax.Precision.HIGHEST)  11.9 us
    ppermute x3, starting transfers between devices, lay_the_joints(): far_arr = jax.lax.ppermute(all_values, axis_name=named_axis, perm=samples)  10.6 us
    another operation x2, other arithmetic, invert(): lax.linalg.triangular_solve(factor, identity, left_side=True, lower=True)  10.5 us
  transfers between devices with their start and end apart: 6, of which 5 were waited for; matrix products, arithmetic and copies ran while one was open for 12% of the time, Pallas kernels for 0%

profile of v1, /device:TPU:0, one launch (start us, length us, event | category | flops | bytes accessed | tf_op | source)
XLA Modules:
  0.0 350.0 jit_solution(6389962338625508100)
XLA Ops:
  7.2 0.7 copy-done
  7.9 0.8 fusion.19
  8.8 4.3 %fusion.18 = f32[8192,128]{1,0:T(8,128)} fusion(bf16[128,8192]{1,0:T(8,128)(2,1)} %param.3, bf16[128,128]{1,0:T(8,128)(2,1)S(1)} %copy-done), kind=kOutput, calls=%fused_computation.49 | convolution fusion | flops 268435456 | bytes 6324224 | tf_op jit(solution)/shard_map/dot_general | solution.py:40
  13.3 70.6 %all-reduce.3.cloned.1.call-done = f32[128,128]{0,1:T(8,128)} async-done(((f32[128,128]{0,1:T(8,128)}), f32[128,128]{0,1:T(8,128)}) %all-reduce.3.cloned.1.call-update) | async-done | bytes 65552 | tf_op jit(solution)/shard_map/psum | solution.py:47
  84.0 0.8 convert_add_fusion
  84.9 11.7 %cholesky.29 = f32[128,128]{1,0:T(8,128)S(1)} custom-call(f32[128,128]{1,0:T(8,128)S(1)} %fusion.14), custom_call_target="Cholesky" | custom-call | tf_op jit(solution)/shard_map/jit(cholesky)/cholesky | solution.py:17
  96.7 0.6 compare_reduce_fusion
  97.3 0.7 fusion.11
  98.0 9.8 %custom-call.6 = f32[1,128,128]{1,2,0:T(8,128)S(1)} custom-call(f32[1,128,128]{2,1,0:T(8,128)S(1)} %fusion.11), custom_call_target="InvertDiagBlocksLowerTriangular" | custom-call | tf_op jit(solution)/shard_map/triangular_solve | solution.py:18
  107.8 0.2 fusion.12
  108.0 0.3 fusion.20
  108.3 67.6 %reduce-scatter.2.cloned.1.call-done = f32[1024,128]{1,0:T(8,128)} async-done(((f32[8192,128]{1,0:T(8,128)}), f32[1024,128]{1,0:T(8,128)}) %reduce-scatter.2.cloned.1.call-update) | async-done | bytes 524304 | tf_op jit(solution)/shard_map/reduce_scatter | solution.py:39
  175.9 2.3 constant_dynamic-update-slice_fusion.7
  178.2 1.6 fusion.21
  179.9 2.4 copy.5
  182.4 3.0 collective-permute-start
  185.3 81.3 %all-reduce.5.cloned.1.call-done = f32[128,128]{1,0:T(8,128)} async-done(((f32[128,128]{1,0:T(8,128)}), f32[128,128]{1,0:T(8,128)}) %all-reduce.5.cloned.1.call-update) | async-done | bytes 65552 | tf_op jit(solution)/shard_map/psum | solution.py:53
  266.7 1.5 select_reduce_fusion
  268.1 1.7 fusion.10
  270.0 2.0 fusion.16
  272.0 0.2 fusion.9
  272.7 0.2 fusion.8
  273.3 0.2 fusion.7
  273.9 0.2 fusion.6
  274.6 0.2 fusion.5
  275.3 5.1 %collective-permute-start.1 = (bf16[2048,128]{1,0:T(8,128)(2,1)S(1)}, bf16[2048,128]{1,0:T(8,128)(2,1)S(1)}, u32[]{:S(2)}, u32[]{:S(2)}) collective-permute-start(bf16[2048,128]{1,0:T(8,128)(2,1)S(1)} %pad_maximum_fusion.1), channel_id=1, source_target_pairs={{0,12},{2,14},{4,0},{6,2},{8,4},{10,6},{12,8},{14,10},{1,13},{3,15... | collective-permute-start | bytes 1572872 | tf_op jit(solution)/shard_map/ppermute | solution.py:67
  281.0 8.4 %collective-permute-done.1 = bf16[2048,128]{1,0:T(8,128)(2,1)S(1)} collective-permute-done((bf16[2048,128]{1,0:T(8,128)(2,1)S(1)}, bf16[2048,128]{1,0:T(8,128)(2,1)S(1)}, u32[]{:S(2)}, u32[]{:S(2)}) %collective-permute-start.1) | collective-permute-done | bytes 524320 | tf_op jit(solution)/shard_map/ppermute | solution.py:67
  289.5 2.6 collective-permute-start.2
  292.5 1.4 fusion.2
  294.0 41.1 %collective-permute-done.2 = bf16[4096,128]{1,0:T(8,128)(2,1)S(1)} collective-permute-done((bf16[4096,128]{1,0:T(8,128)(2,1)S(1)}, bf16[4096,128]{1,0:T(8,128)(2,1)S(1)}, u32[]{:S(2)}, u32[]{:S(2)}) %collective-permute-start.2) | collective-permute-done | bytes 1048608 | tf_op jit(solution)/shard_map/ppermute | solution.py:67
  335.5 5.0 %subtract_convert_fusion = bf16[128,8192]{0,1:T(8,128)(2,1)S(1)} fusion(bf16[128,128]{1,0:T(8,128)(2,1)S(1)} %copy-done, bf16[128,8192]{0,1:T(8,128)(2,1)S(1)} %copy-done.2, f32[8192]{0:T(1024)S(1)} %broadcast_add_fusion, f32[8192]{0:T(1024)S(1)} %copy-done.3, bf16[16384,128]{1,0:T(8,128)(2,1)S(1)} %constant_dynamic-update-slice_fusion, s32[]{:T(128)S(6)} %select_n.24), kind=kOutput, calls=%fused_computation.2 | convolution fusion | flops 274726912 | bytes 6389764 | tf_op jit(solution)/shard_map/dot_general | solution.py:72
  340.6 2.9 copy.9
  (47 shorter events, 4.3 us)
Async XLA Ops:
  7.2 0.8 copy-start
  7.2 76.8 %all-reduce.3.cloned.1.call-start = ((), (), s32[]{:S(2)}) async-start(), calls=%async_computation.2 | async-start | bytes 131072 | tf_op jit(solution)/shard_map/psum | solution.py:47
  8.8 167.1 %reduce-scatter.2.cloned.1.call-start = ((), (), s32[]{:S(2)}) async-start(), calls=%async_computation.1 | async-start | bytes 4718592 | tf_op jit(solution)/shard_map/reduce_scatter | solution.py:39
  13.1 166.8 %copy-start.3 = (f32[8192]{0:T(1024)S(1)}, f32[8192]{0:T(1024)}, u32[]{:S(2)}) copy-start(f32[8192]{0:T(1024)} %param.5) | copy-start | bytes 98308
  13.1 166.8 %copy-start.1 = (bf16[128,8192]{1,0:T(8,128)(2,1)S(1)}, bf16[128,8192]{1,0:T(8,128)(2,1)}, u32[]{:S(2)}) copy-start(bf16[128,8192]{1,0:T(8,128)(2,1)} %param.3) | copy-start | bytes 6291460
  13.2 253.5 %all-reduce.5.cloned.1.call-start = ((), (), s32[]{:S(2)}) async-start(), calls=%async_computation.3 | async-start | bytes 131072 | tf_op jit(solution)/shard_map/psum | solution.py:53
  182.4 92.8 %collective-permute-start = (bf16[1024,128]{1,0:T(8,128)(2,1)S(1)}, bf16[1024,128]{1,0:T(8,128)(2,1)S(1)}, u32[]{:S(2)}, u32[]{:S(2)}) collective-permute-start(bf16[1024,128]{1,0:T(8,128)(2,1)S(1)} %get-tuple-element.5), channel_id=1, source_target_pairs={{0,14},{2,0},{4,2},{6,4},{8,6},{10,8},{12,10},{14,12},{1,15},{3,1}... | collective-permute-start | bytes 786440 | tf_op jit(solution)/shard_map/ppermute | solution.py:67
  270.0 23.8 %copy-start.4 = (bf16[16384,128]{1,0:T(8,128)(2,1)S(1)}, bf16[16384,128]{1,0:T(8,128)(2,1)}, u32[]{:S(2)}) copy-start(bf16[16384,128]{1,0:T(8,128)(2,1)} %get-tuple-element.4) | copy-start | bytes 12582916
  275.3 14.2 %collective-permute-start.1 = (bf16[2048,128]{1,0:T(8,128)(2,1)S(1)}, bf16[2048,128]{1,0:T(8,128)(2,1)S(1)}, u32[]{:S(2)}, u32[]{:S(2)}) collective-permute-start(bf16[2048,128]{1,0:T(8,128)(2,1)S(1)} %pad_maximum_fusion.1), channel_id=1, source_target_pairs={{0,12},{2,14},{4,0},{6,2},{8,4},{10,6},{12,8},{14,10},{1,13},{3,15... | collective-permute-start | bytes 1572872 | tf_op jit(solution)/shard_map/ppermute | solution.py:67
  289.5 45.6 %collective-permute-start.2 = (bf16[4096,128]{1,0:T(8,128)(2,1)S(1)}, bf16[4096,128]{1,0:T(8,128)(2,1)S(1)}, u32[]{:S(2)}, u32[]{:S(2)}) collective-permute-start(bf16[4096,128]{1,0:T(8,128)(2,1)S(1)} %pad_maximum_fusion), channel_id=1, source_target_pairs={{0,8},{2,10},{4,12},{6,14},{8,0},{10,2},{12,4},{14,6},{1,9},{3,11}... | collective-permute-start | bytes 3145736 | tf_op jit(solution)/shard_map/ppermute | solution.py:67
  293.8 41.7 %copy-start.2 = (bf16[128,8192]{0,1:T(8,128)(2,1)S(1)}, bf16[128,8192]{0,1:T(8,128)(2,1)}, u32[]{:S(2)}) copy-start(bf16[128,8192]{0,1:T(8,128)(2,1)} %copy.5) | copy-start | bytes 6291460
Sparse Core Ops, SparseCore 0:
  12.0 71.9 all-reduce.2
  87.6 88.2 reduce-scatter.1
  180.0 86.6 all-reduce.4

commit v2 on v0

--- a/solution.py
+++ b/solution.py
@@ -6,6 +6,7 @@
 
 NS_STEPS = 8
 shrink_rate = 0.25
+_form_sector = lambda here_x: jnp.sum(jax.lax.all_gather(here_x, ("cell", "gene")), 0)
 
 
 def matmul(left, right):
@@ -50,7 +51,7 @@
     local_moment = lax.dot_general(
         coef, coef, (((0,), (0,)), ((), ())), precision=lax.Precision.HIGHEST
     )
-    moment = lax.psum(local_moment, ("cell", "gene"))
+    moment = _form_sector(local_moment)
     root_inv = newton(moment)
     low_rank_coef = coef - shrink_rate / math.sqrt(width) * matmul(coef, root_inv)
     coef_low = coef.astype(jnp.bfloat16)

time: 336 us -> 285 us (0.85)
  waiting for transfers between devices: 264 us -> 214 us
    psum x1 -> x0, waiting for transfers between devices: 83.3 us -> none  [per_device(): moment = lax.psum(local_moment, ('cell', 'gene'))]
    all_gather x0 -> x1, waiting for transfers between devices: none -> 34.9 us  [jax.lax.all_gather(here_x, ('cell', 'gene'))]
  transfers between devices with their start and end apart: 4 -> 4, of which waited for: 4 -> 4; matrix products, arithmetic and copies ran while one was open for 12% -> 14% of each run, Pallas kernels for 0% -> 0%
where the time goes in v2:
time: 285 us
  waiting for transfers between devices  214 us (75%)
  other arithmetic  25.6 us (9%)
  matrix products  23.1 us (8%)
  between operations  14 us (5%)
  local copies, waits for them, and re-layouts  7.44 us (3%)
    psum x1, waiting for transfers between devices, per_device(): gram_total = lax.psum(local_gram, 'cell')  70.6 us
    reduce_scatter x1, waiting for transfers between devices, per_device(): lax.psum_scatter(lax.dot_general(expression, design, (((0,), (0,)), ((),...  67.6 us
    all_gather x1, waiting for transfers between devices, per_device(): lax.all_gather(coef_low, 'cell', axis=0, tiled=True)  40.8 us
    all_gather x1, waiting for transfers between devices, jax.lax.all_gather(here_x, ('cell', 'gene'))  34.9 us
    another operation x4, other arithmetic, invert(): factor = jnp.linalg.cholesky(matrix)  12.4 us
    another operation x2, other arithmetic, invert(): lax.linalg.triangular_solve(factor, identity, left_side=True, lower=True)  10.5 us
    dot_general x26, matrix products, matmul(): return jnp.dot(left, right, precision=lax.Precision.HIGHEST)  9.95 us
    unnamed x10, local copies, waits for them, and re-layouts  7.23 us
  transfers between devices with their start and end apart: 4, of which 4 were waited for; matrix products, arithmetic and copies ran while one was open for 14% of the time, Pallas kernels for 0%

profile of v2, /device:TPU:0, one launch (start us, length us, event | category | flops | bytes accessed | tf_op | source)
XLA Modules:
  0.0 284.5 jit_solution(5698593669830499091)
XLA Ops:
  7.2 0.7 copy-done
  7.9 0.8 fusion.18
  8.8 4.3 %fusion.17 = f32[8192,128]{1,0:T(8,128)} fusion(bf16[128,8192]{1,0:T(8,128)(2,1)} %param.3, bf16[128,128]{1,0:T(8,128)(2,1)S(1)} %copy-done), kind=kOutput, calls=%fused_computation.38 | convolution fusion | flops 268435456 | bytes 6324224 | tf_op jit(solution)/shard_map/dot_general | solution.py:41
  13.3 70.6 %all-reduce.2.cloned.1.call-done = f32[128,128]{0,1:T(8,128)} async-done(((f32[128,128]{0,1:T(8,128)}), f32[128,128]{0,1:T(8,128)}) %all-reduce.2.cloned.1.call-update) | async-done | bytes 65552 | tf_op jit(solution)/shard_map/psum | solution.py:48
  84.0 0.8 convert_add_fusion
  84.9 11.7 %cholesky.29 = f32[128,128]{1,0:T(8,128)S(1)} custom-call(f32[128,128]{1,0:T(8,128)S(1)} %fusion.13), custom_call_target="Cholesky" | custom-call | tf_op jit(solution)/shard_map/jit(cholesky)/cholesky | solution.py:18
  96.7 0.6 compare_reduce_fusion
  97.3 0.7 fusion.10
  98.0 9.8 %custom-call.6 = f32[1,128,128]{1,2,0:T(8,128)S(1)} custom-call(f32[1,128,128]{2,1,0:T(8,128)S(1)} %fusion.10), custom_call_target="InvertDiagBlocksLowerTriangular" | custom-call | tf_op jit(solution)/shard_map/triangular_solve | solution.py:19
  107.8 0.2 fusion.11
  108.0 0.3 fusion.19
  108.3 67.6 %reduce-scatter.2.cloned.1.call-done = f32[1024,128]{1,0:T(8,128)} async-done(((f32[8192,128]{1,0:T(8,128)}), f32[1024,128]{1,0:T(8,128)}) %reduce-scatter.2.cloned.1.call-update) | async-done | bytes 524304 | tf_op jit(solution)/shard_map/reduce_scatter | solution.py:40
  176.0 2.3 fusion.16
  178.3 1.6 fusion.20
  180.0 0.2 all-gather.4.cloned.1.call-start
  180.2 2.4 copy.5
  182.7 34.9 %all-gather.6.cloned.1.call-done = f32[2048,128]{1,0:T(8,128)} async-done(((f32[128,128]{1,0:T(8,128)}), f32[2048,128]{1,0:T(8,128)}) %all-gather.6.cloned.1.call-update) | async-done | bytes 1048592 | tf_op jit(solution)/shard_map/all_gather | solution.py:9
  217.6 1.3 reduce_sum.19
  218.9 0.6 select_reduce_fusion
  219.5 0.8 fusion.9
  220.5 0.8 fusion.15
  221.4 0.2 fusion.8
  221.6 0.2 fusion.21
  222.0 0.2 fusion.7
  222.2 0.2 fusion.23
  222.4 0.2 fusion.24
  222.7 0.2 fusion.6
  223.3 0.2 fusion.5
  225.6 1.4 fusion.1
  227.0 40.8 %all-gather.4.cloned.1.call-done = bf16[8192,128]{1,0:T(8,128)(2,1)} async-done(((bf16[1024,128]{1,0:T(8,128)(2,1)}), bf16[8192,128]{1,0:T(8,128)(2,1)}) %all-gather.4.cloned.1.call-update) | async-done | bytes 2097168 | tf_op jit(solution)/shard_map/all_gather | solution.py:60
  267.8 6.2 %subtract_convert_fusion = bf16[128,8192]{0,1:T(8,128)(2,1)} fusion(bf16[8192,128]{1,0:T(8,128)(2,1)} %all-gather.4.cloned.1.call-done, bf16[128,128]{1,0:T(8,128)(2,1)S(1)} %copy-done, bf16[128,8192]{0,1:T(8,128)(2,1)S(1)} %copy-done.2, f32[8192]{0:T(1024)S(1)} %broadcast_add_fusion, f32[8192]{0:T(1024)S(1)} %copy-done.3), kind=kOutput, calls=%fused_computation.2 | convolution fusion | flops 274726912 | bytes 6389760 | tf_op jit(solution)/shard_map/dot_general | solution.py:58
  273.9 4.1 %copy.9 = bf16[128,8192]{1,0:T(8,128)(2,1)} copy(bf16[128,8192]{0,1:T(8,128)(2,1)} %subtract_convert_fusion) | data formatting | bytes 4194304
  (34 shorter events, 3.3 us)
Async XLA Ops:
  7.2 0.8 copy-start
  7.2 76.8 %all-reduce.2.cloned.1.call-start = ((), (), s32[]{:S(2)}) async-start(), calls=%async_computation.2 | async-start | bytes 131072 | tf_op jit(solution)/shard_map/psum | solution.py:48
  8.8 167.2 %reduce-scatter.2.cloned.1.call-start = ((), (), s32[]{:S(2)}) async-start(), calls=%async_computation.1 | async-start | bytes 4718592 | tf_op jit(solution)/shard_map/reduce_scatter | solution.py:40
  13.1 167.1 %copy-start.1 = (bf16[128,8192]{1,0:T(8,128)(2,1)S(1)}, bf16[128,8192]{1,0:T(8,128)(2,1)}, u32[]{:S(2)}) copy-start(bf16[128,8192]{1,0:T(8,128)(2,1)} %param.3) | copy-start | bytes 6291460
  13.2 204.4 %all-gather.6.cloned.1.call-start = ((), (), s32[]{:S(2)}) async-start(), calls=%async_computation.4 | async-start | bytes 1114112 | tf_op jit(solution)/shard_map/all_gather | solution.py:9
  179.9 2.7 copy-start.3
  180.0 87.8 %all-gather.4.cloned.1.call-start = ((), (), s32[]{:S(2)}) async-start(), calls=%async_computation.3 | async-start | bytes 2359296 | tf_op jit(solution)/shard_map/all_gather | solution.py:60
  222.2 45.5 %copy-start.2 = (bf16[128,8192]{0,1:T(8,128)(2,1)S(1)}, bf16[128,8192]{0,1:T(8,128)(2,1)}, u32[]{:S(2)}) copy-start(bf16[128,8192]{0,1:T(8,128)(2,1)} %copy.5) | copy-start | bytes 6291460
Sparse Core Ops, SparseCore 0:
  12.0 71.9 all-reduce.1
  87.6 88.3 reduce-scatter.1
  180.1 37.4 all-gather.5
  219.6 48.1 all-gather.3
